TPU v7x, 512 devices: a whole 4x4x16 slice. The times are simulated.
512 devices in a mesh: dp: 8 (over x_hi, y), tm: 64 (over x_lo, z, core).
Axes of the slice: x: 4 (x_hi: 2, x_lo: 2; x = x_hi * 2 + x_lo), y: 4, z: 16, core: 2. Of those that a mesh axis runs over, the one named last changes fastest.
Arguments:
- signal: bfloat16 [8, 65536, 256], P('dp', 'tm'), may hold values from -6 to 6
- cotangent: bfloat16 [8, 65536, 256], P('dp', 'tm'), may hold values from -6 to 6
- first_history_weight: bfloat16 [256, 512], replicated, may hold values from -0.25 to 0.25
- first_current_weight: bfloat16 [256, 512], replicated, may hold values from -0.25 to 0.25
- first_residual_weight: bfloat16 [256, 256], replicated, may hold values from -0.375 to 0.375
- second_history_weight: bfloat16 [256, 512], replicated, may hold values from -0.25 to 0.25
- second_current_weight: bfloat16 [256, 512], replicated, may hold values from -0.25 to 0.25
- second_residual_weight: bfloat16 [256, 256], replicated, may hold values from -0.375 to 0.375
Outputs:
- grad_signal: bfloat16 [8, 65536, 256], P('dp', 'tm')
- grad_past_one: bfloat16 [256, 512], replicated
- grad_now_one: bfloat16 [256, 512], replicated
- grad_mix_one: bfloat16 [256, 256], replicated
- grad_past_two: bfloat16 [256, 512], replicated
- grad_now_two: bfloat16 [256, 512], replicated
- grad_mix_two: bfloat16 [256, 256], replicated
All inputs are finite; a program needn't handle non-finite values.
Results may differ from a plain program's by a relative error of at most 0.0068.
Values may be sent and summed in bfloat16 or wider, within the bound.
No kernel may reach another device: no remote copies, remote signals or barrier semaphores. Data moves between devices by JAX's collectives and lax.ppermute only.
A program may use at most 64 MiB of HBM per device.

v0:
```python
import math
import jax
import jax.numpy as jnp
from jax import lax
from jax.sharding import PartitionSpec as P

FIRST_DILATION = 512
SECOND_DILATION = 8192


def shifted(value, axis, steps):
    count = lax.axis_size(axis)
    leading, last = (max(0, -steps), min(count, count - steps))
    return lax.ppermute(value, axis, [(source, source + steps) for source in range(leading, last)])


def forward_layer(input_traces, past_rows, tap_past, tap_now, mixing):
    channels = input_traces.shape[-1]
    flat_now = input_traces.reshape(-1, channels)
    flat_past = past_rows.reshape(-1, channels)
    pre_act = jnp.dot(flat_past, tap_past, preferred_element_type=jnp.float32) + jnp.dot(
        flat_now, tap_now, preferred_element_type=jnp.float32
    )
    half_width = pre_act.shape[1] // 2
    filter_part = jnp.tanh(pre_act[:, :half_width])
    gate_part = jax.nn.sigmoid(pre_act[:, half_width:])
    hidden = (filter_part * gate_part).astype(jnp.bfloat16)
    output = (
        flat_now.astype(jnp.float32) + jnp.dot(hidden, mixing, preferred_element_type=jnp.float32)
    ).astype(jnp.bfloat16)
    return (filter_part, gate_part, hidden, output.reshape(input_traces.shape))


def backward_layer(input_traces, past_rows, saved, incoming_gradient, tap_past, tap_now, mixing):
    filter_part, gate_part, hidden, output = saved
    channels = input_traces.shape[-1]
    flat_now = input_traces.reshape(-1, channels)
    flat_past = past_rows.reshape(-1, channels)
    flat_up = incoming_gradient.reshape(-1, channels)
    hidden_grad = jnp.dot(flat_up, mixing.T, preferred_element_type=jnp.float32)
    filter_grad = hidden_grad * gate_part * (1.0 - filter_part * filter_part)
    gate_grad = hidden_grad * filter_part * gate_part * (1.0 - gate_part)
    pre_grad = jnp.concatenate([filter_grad, gate_grad], axis=1).astype(jnp.bfloat16)
    past_term = jnp.einsum("rc,rg->cg", flat_past, pre_grad, preferred_element_type=jnp.float32)
    now_term = jnp.einsum("rc,rg->cg", flat_now, pre_grad, preferred_element_type=jnp.float32)
    mix_term = jnp.einsum("rh,rc->hc", hidden, flat_up, preferred_element_type=jnp.float32)
    ahead_rows = (
        jnp.dot(pre_grad, tap_past.T, preferred_element_type=jnp.float32)
        .astype(jnp.bfloat16)
        .reshape(input_traces.shape)
    )
    local_grad = (
        flat_up.astype(jnp.float32)
        + jnp.dot(pre_grad, tap_now.T, preferred_element_type=jnp.float32)
    ).reshape(input_traces.shape)
    return (local_grad, ahead_rows, (past_term, now_term, mix_term))


def reduce_grads(term_list, scale_factor):
    past_term, now_term, mix_term = term_list
    summed = lax.psum((past_term, now_term, mix_term), ("dp", "tm"))
    return tuple(((member * scale_factor).astype(jnp.bfloat16) for member in summed))


def body(
    signal,
    cotangent,
    first_history_weight,
    first_current_weight,
    first_residual_weight,
    second_history_weight,
    second_current_weight,
    second_residual_weight,
):
    seq_count, number_of_steps, channels = signal.shape
    rows_all = seq_count * lax.axis_size("dp") * number_of_steps * lax.axis_size("tm")
    scale_factor = 1.0 / math.sqrt(rows_all)
    final_rows = signal[:, number_of_steps - FIRST_DILATION :, :]
    received_rows = shifted(final_rows, "tm", 1)
    first_history_rows = jnp.concatenate(
        [received_rows, signal[:, : number_of_steps - FIRST_DILATION, :]], axis=1
    )
    first_layer_stash = forward_layer(
        signal,
        first_history_rows,
        first_history_weight,
        first_current_weight,
        first_residual_weight,
    )
    hidden_activation = first_layer_stash[3]
    distant_offsets = SECOND_DILATION // number_of_steps
    past_two = shifted(hidden_activation, "tm", distant_offsets)
    second_layer_stash = forward_layer(
        hidden_activation,
        past_two,
        second_history_weight,
        second_current_weight,
        second_residual_weight,
    )
    local_two, ahead_two, second_layer_terms = backward_layer(
        hidden_activation,
        past_two,
        second_layer_stash,
        cotangent,
        second_history_weight,
        second_current_weight,
        second_residual_weight,
    )
    arrived_back = shifted(ahead_two, "tm", -distant_offsets)
    hidden_gradient = (local_two + arrived_back.astype(jnp.float32)).astype(jnp.bfloat16)
    reduced_two = reduce_grads(second_layer_terms, scale_factor)
    local_one, forward_rows_first, first_layer_terms = backward_layer(
        signal,
        first_history_rows,
        first_layer_stash,
        hidden_gradient,
        first_history_weight,
        first_current_weight,
        first_residual_weight,
    )
    leading_rows = forward_rows_first[:, :FIRST_DILATION, :]
    received_head_rows = shifted(leading_rows, "tm", -1)
    trailing_later_rows = jnp.concatenate(
        [forward_rows_first[:, FIRST_DILATION:, :], received_head_rows], axis=1
    )
    grad_signal = (local_one + trailing_later_rows.astype(jnp.float32)).astype(jnp.bfloat16)
    reduced_one = reduce_grads(first_layer_terms, scale_factor)
    return (
        grad_signal,
        reduced_one[0],
        reduced_one[1],
        reduced_one[2],
        reduced_two[0],
        reduced_two[1],
        reduced_two[2],
    )


def solution(mesh):
    in_specs = (P("dp", "tm", None), P("dp", "tm", None), P(), P(), P(), P(), P(), P())
    out_specs = (P("dp", "tm", None), P(), P(), P(), P(), P(), P())
    return jax.shard_map(body, mesh=mesh, in_specs=in_specs, out_specs=out_specs, check_vma=False)
```

profile of v0, /device:TPU:2, one launch (start us, length us, event | category | flops | bytes accessed | tf_op | source)
XLA Modules:
  0.0 616.3 jit_solution(2754087225272459337)
XLA Ops:
  7.2 0.0 copy-start
  7.2 0.0 copy-start.4
  7.2 0.0 all-reduce.3.cloned.1.call-start
  7.2 1.1 fusion.28
  8.4 1.9 collective-permute-start
  10.3 1.6 fusion.17
  11.9 11.3 %collective-permute-done = bf16[1,512,256]{2,1,0:T(8,128)(2,1)S(1)} collective-permute-done((bf16[1,512,256]{2,1,0:T(8,128)(2,1)S(1)}, bf16[1,512,256]{2,1,0:T(8,128)(2,1)S(1)}, u32[]{:S(2)}, u32[]{:S(2)}) %collective-permute-start) | collective-permute-done | bytes 262176 | tf_op jit(solution)/shard_map/ppermute | solution.py:14
  23.2 0.0 copy-done.4
  23.2 0.5 convolution_add_fusion.1
  23.7 0.0 copy-start.1
  23.7 0.0 copy-start.7
  23.8 0.0 copy-start.5
  23.8 0.4 multiply_convert_fusion.5
  24.2 0.6 copy-done.1
  24.8 0.0 copy-done.7
  24.8 0.4 fusion.1
  25.2 3.1 collective-permute-start.1
  28.3 0.0 copy-done.5
  28.3 0.5 fusion.29
  28.8 0.0 copy-start.8
  28.8 0.0 copy-start.9
  28.8 23.2 %collective-permute-done.1 = bf16[1,1024,256]{2,1,0:T(8,128)(2,1)S(1)} collective-permute-done((bf16[1,1024,256]{2,1,0:T(8,128)(2,1)S(1)}, bf16[1,1024,256]{2,1,0:T(8,128)(2,1)S(1)}, u32[]{:S(2)}, u32[]{:S(2)}) %collective-permute-start.1) | collective-permute-done | bytes 524320 | tf_op jit(solution)/shard_map/ppermute | solution.py:14
  52.0 0.0 copy-done
  52.0 0.5 convolution_add_fusion
  52.5 0.0 copy-done.8
  52.5 0.0 copy-done.9
  52.5 0.7 multiply_convert_fusion.4
  53.2 1.3 fusion.26
  54.5 0.5 fusion.2
  55.0 8.9 %collective-permute-start.2 = (bf16[1,1024,256]{2,1,0:T(8,128)(2,1)S(1)}, bf16[1,1024,256]{2,1,0:T(8,128)(2,1)S(1)}, u32[]{:S(2)}, u32[]{:S(2)}) collective-permute-start(bf16[1,1024,256]{2,1,0:T(8,128)(2,1)S(1)} %fusion.2), channel_id=1, source_target_pairs={{8,0},{9,1},{10,2},{11,3},{12,4},{13,5},{14,6},{15,7},{16,8},{17,9... | collective-permute-start | bytes 1572872 | tf_op jit(solution)/shard_map/ppermute | solution.py:14
  64.0 1.3 fusion.13
  65.2 1.3 fusion.12
  66.5 30.5 %collective-permute-done.2 = bf16[1,1024,256]{2,1,0:T(8,128)(2,1)S(1)} collective-permute-done((bf16[1,1024,256]{2,1,0:T(8,128)(2,1)S(1)}, bf16[1,1024,256]{2,1,0:T(8,128)(2,1)S(1)}, u32[]{:S(2)}, u32[]{:S(2)}) %collective-permute-start.2) | collective-permute-done | bytes 524320 | tf_op jit(solution)/shard_map/ppermute | solution.py:14
  97.0 0.5 fusion.10
  97.5 0.7 multiply_convert_fusion.2
  98.2 1.0 fusion.30
  99.2 1.3 convolution_bitcast_fusion
  100.5 1.3 fusion.22
  101.7 0.0 all-reduce.3.cloned.1.call-update
  101.8 0.0 copy-start.6
  101.8 0.5 fusion.3
  102.3 13.7 %collective-permute-start.3 = (bf16[1,512,256]{2,1,0:T(8,128)(2,1)S(1)}, bf16[1,512,256]{2,1,0:T(8,128)(2,1)S(1)}, u32[]{:S(2)}, u32[]{:S(2)}) collective-permute-start(bf16[1,512,256]{2,1,0:T(8,128)(2,1)S(1)} %get-tuple-element.18), channel_id=1, source_target_pairs={{1,0},{2,1},{3,2},{4,3},{5,4},{6,5},{7,6},{8,7},{9,8},{10,9},{11,1... | collective-permute-start | bytes 786440 | tf_op jit(solution)/shard_map/ppermute | solution.py:14
  116.1 3.9 collective-permute-done.3
  119.9 1.3 fusion.11
  121.2 483.3 %all-reduce.3.cloned.1.call-done = (f32[256,512]{1,0:T(8,128)}, f32[256,512]{1,0:T(8,128)}, f32[256,256]{1,0:T(8,128)}, f32[256,512]{1,0:T(8,128)}, f32[256,512]{1,0:T(8,128)}, /*index=5*/f32[256,256]{1,0:T(8,128)}) async-done(((f32[256,512]{1,0:T(8,128)}, f32[256,512]{1,0:T(8,128)}, f32[256,256]{1,0:T(8,128)}, f32[256,512]{1,0:T(8,128)}, f32[256,512]{1,0:T(8,128)}, /*index=5*/f32[256,256]{1,0:T(8,128)}), ...) | async-done | bytes 2621456 | tf_op jit(solution)/shard_map/psum | solution.py:61
  604.5 2.2 multiply_convert_fusion.9
  606.7 1.8 multiply_convert_fusion.11
  608.5 0.9 multiply_convert_fusion.7
  (6 shorter events, 0.0 us)
Async XLA Ops:
  7.2 44.8 %copy-start = (bf16[256,512]{1,0:T(8,128)(2,1)S(1)}, bf16[256,512]{1,0:T(8,128)(2,1)}, u32[]{:S(2)}) copy-start(bf16[256,512]{1,0:T(8,128)(2,1)} %param.13) | copy-start | bytes 786436
  7.2 16.1 %copy-start.4 = (bf16[256,512]{1,0:T(8,128)(2,1)S(1)}, bf16[256,512]{1,0:T(8,128)(2,1)}, u32[]{:S(2)}) copy-start(bf16[256,512]{1,0:T(8,128)(2,1)} %param.10) | copy-start | bytes 786436
  7.2 597.3 %all-reduce.3.cloned.1.call-start = ((), (), s32[]{:S(2)}) async-start(), calls=%async_computation | async-start | bytes 5242880 | tf_op jit(solution)/shard_map/psum | solution.py:61
  8.4 14.9 %collective-permute-start = (bf16[1,512,256]{2,1,0:T(8,128)(2,1)S(1)}, bf16[1,512,256]{2,1,0:T(8,128)(2,1)S(1)}, u32[]{:S(2)}, u32[]{:S(2)}) collective-permute-start(bf16[1,512,256]{2,1,0:T(8,128)(2,1)S(1)} %get-tuple-element.19), channel_id=1, source_target_pairs={{0,1},{1,2},{2,3},{3,4},{4,5},{5,6},{6,7},{7,8},{8,9},{9,10},{10,1... | collective-permute-start | bytes 786440 | tf_op jit(solution)/shard_map/ppermute | solution.py:14
  23.7 1.0 copy-start.1
  23.7 1.1 copy-start.7
  23.8 4.5 copy-start.5
  25.2 26.8 %collective-permute-start.1 = (bf16[1,1024,256]{2,1,0:T(8,128)(2,1)S(1)}, bf16[1,1024,256]{2,1,0:T(8,128)(2,1)S(1)}, u32[]{:S(2)}, u32[]{:S(2)}) collective-permute-start(bf16[1,1024,256]{2,1,0:T(8,128)(2,1)S(1)} %bitcast.60), channel_id=1, source_target_pairs={{0,8},{1,9},{2,10},{3,11},{4,12},{5,13},{6,14},{7,15},{8,16},{9,17... | collective-permute-start | bytes 1572872 | tf_op jit(solution)/shard_map/ppermute | solution.py:14
  28.8 23.7 %copy-start.8 = (bf16[1,1024,256]{2,1,0:T(8,128)(2,1)S(1)}, bf16[1,1024,256]{2,1,0:T(8,128)(2,1)}, u32[]{:S(2)}) copy-start(bf16[1,1024,256]{2,1,0:T(8,128)(2,1)} %param.9) | copy-start | bytes 1572868
  28.8 23.7 %copy-start.9 = (bf16[256,256]{1,0:T(8,128)(2,1)S(1)}, bf16[256,256]{1,0:T(8,128)(2,1)}, u32[]{:S(2)}) copy-start(bf16[256,256]{1,0:T(8,128)(2,1)} %param.15) | copy-start | bytes 393220
  55.0 42.0 %collective-permute-start.2 = (bf16[1,1024,256]{2,1,0:T(8,128)(2,1)S(1)}, bf16[1,1024,256]{2,1,0:T(8,128)(2,1)S(1)}, u32[]{:S(2)}, u32[]{:S(2)}) collective-permute-start(bf16[1,1024,256]{2,1,0:T(8,128)(2,1)S(1)} %fusion.2), channel_id=1, source_target_pairs={{8,0},{9,1},{10,2},{11,3},{12,4},{13,5},{14,6},{15,7},{16,8},{17,9... | collective-permute-start | bytes 1572872 | tf_op jit(solution)/shard_map/ppermute | solution.py:14
  101.8 18.2 %copy-start.6 = (bf16[256,512]{1,0:T(8,128)(2,1)S(1)}, bf16[256,512]{1,0:T(8,128)(2,1)}, u32[]{:S(2)}) copy-start(bf16[256,512]{1,0:T(8,128)(2,1)} %param.11) | copy-start | bytes 786436
  102.3 17.6 %collective-permute-start.3 = (bf16[1,512,256]{2,1,0:T(8,128)(2,1)S(1)}, bf16[1,512,256]{2,1,0:T(8,128)(2,1)S(1)}, u32[]{:S(2)}, u32[]{:S(2)}) collective-permute-start(bf16[1,512,256]{2,1,0:T(8,128)(2,1)S(1)} %get-tuple-element.18), channel_id=1, source_target_pairs={{1,0},{2,1},{3,2},{4,3},{5,4},{6,5},{7,6},{8,7},{9,8},{10,9},{11,1... | collective-permute-start | bytes 786440 | tf_op jit(solution)/shard_map/ppermute | solution.py:14
  604.5 4.0 copy-start.2
  604.5 4.0 copy-start.3
Sparse Core Ops, SparseCore 0:
  101.9 502.5 all-reduce.2
where the time goes:
time: 617 us; the launch traced here: 616 us
  waiting for transfers between devices  552 us (89%)
  starting transfers between devices  27.8 us (5%)
  matrix products  14.9 us (2%)
  between operations  14.2 us (2%)
    psum x1, waiting for transfers between devices, reduce_grads(): summed = lax.psum((past_term, now_term, mix_term), ('dp', 'tm'))  483 us
    ppermute x4, waiting for transfers between devices, shifted(): lax.ppermute(value, axis, [(source, source + steps) for source in range(l...  68.9 us
    ppermute x4, starting transfers between devices, shifted(): lax.ppermute(value, axis, [(source, source + steps) for source in range(l...  27.7 us
  transfers between devices with their start and end apart: 5, of which 5 were waited for; matrix products, arithmetic and copies ran while one was open for 1% of the time, Pallas kernels for 0%

commit v1 on v0

--- a/solution.py
+++ b/solution.py
@@ -58,7 +58,7 @@
 
 def reduce_grads(term_list, scale_factor):
     past_term, now_term, mix_term = term_list
-    summed = lax.psum((past_term, now_term, mix_term), ("dp", "tm"))
+    summed = lax.psum(lax.psum((past_term, now_term, mix_term), "tm"), "dp")
     return tuple(((member * scale_factor).astype(jnp.bfloat16) for member in summed))
 
 

time: 617 us -> 683 us (1.11)
  the two profiles are of different devices: /device:TPU:2 before, /device:TPU:32 now
where the time goes in v1:
time: 683 us; the launch traced here: 682 us
  waiting for transfers between devices  631 us (92%)
  starting transfers between devices  15.5 us (2%)
  matrix products  15 us (2%)
  between operations  14.3 us (2%)
    psum x2, waiting for transfers between devices, reduce_grads(): summed = lax.psum(lax.psum((past_term, now_term, mix_term), 'tm'), 'dp')  573 us
    ppermute x4, waiting for transfers between devices, shifted(): lax.ppermute(value, axis, [(source, source + steps) for source in range(l...  57.7 us
    ppermute x4, starting transfers between devices, shifted(): lax.ppermute(value, axis, [(source, source + steps) for source in range(l...  15.5 us
  transfers between devices with their start and end apart: 6, of which 6 were waited for; matrix products, arithmetic and copies ran while one was open for 1% of the time, Pallas kernels for 0%

profile of v1, /device:TPU:32, one launch (start us, length us, event | category | flops | bytes accessed | tf_op | source)
XLA Modules:
  0.0 682.4 jit_solution(10499305760429684277)
XLA Ops:
  7.2 0.0 copy-start
  7.2 0.0 copy-start.4
  7.2 0.0 all-reduce.5.cloned.1.call-start
  7.2 1.1 fusion.28
  8.4 1.9 collective-permute-start
  10.3 1.6 fusion.17
  11.9 4.2 collective-permute-done
  16.1 0.0 copy-done.4
  16.1 0.5 convolution_add_fusion.1
  16.6 0.0 copy-start.1
  16.6 0.0 copy-start.7
  16.6 0.0 copy-start.5
  16.6 0.4 multiply_convert_fusion.5
  17.0 0.6 copy-done.1
  17.6 0.0 copy-done.7
  17.6 0.4 fusion.1
  18.0 9.1 %collective-permute-start.1 = (bf16[1,1024,256]{2,1,0:T(8,128)(2,1)S(1)}, bf16[1,1024,256]{2,1,0:T(8,128)(2,1)S(1)}, u32[]{:S(2)}, u32[]{:S(2)}) collective-permute-start(bf16[1,1024,256]{2,1,0:T(8,128)(2,1)S(1)} %bitcast.60), channel_id=1, source_target_pairs={{0,8},{1,9},{2,10},{3,11},{4,12},{5,13},{6,14},{7,15},{8,16},{9,17... | collective-permute-start | bytes 1572872 | tf_op jit(solution)/shard_map/ppermute | solution.py:14
  27.1 0.5 fusion.29
  27.6 0.0 copy-start.8
  27.6 0.0 copy-start.9
  27.6 32.9 %collective-permute-done.1 = bf16[1,1024,256]{2,1,0:T(8,128)(2,1)S(1)} collective-permute-done((bf16[1,1024,256]{2,1,0:T(8,128)(2,1)S(1)}, bf16[1,1024,256]{2,1,0:T(8,128)(2,1)S(1)}, u32[]{:S(2)}, u32[]{:S(2)}) %collective-permute-start.1) | collective-permute-done | bytes 524320 | tf_op jit(solution)/shard_map/ppermute | solution.py:14
  60.6 0.5 convolution_add_fusion
  61.1 0.7 multiply_convert_fusion.4
  61.8 1.3 fusion.26
  63.1 0.5 fusion.2
  63.6 1.3 collective-permute-start.2
  64.9 1.3 fusion.13
  66.2 1.3 fusion.12
  67.4 16.8 %collective-permute-done.2 = bf16[1,1024,256]{2,1,0:T(8,128)(2,1)S(1)} collective-permute-done((bf16[1,1024,256]{2,1,0:T(8,128)(2,1)S(1)}, bf16[1,1024,256]{2,1,0:T(8,128)(2,1)S(1)}, u32[]{:S(2)}, u32[]{:S(2)}) %collective-permute-start.2) | collective-permute-done | bytes 524320 | tf_op jit(solution)/shard_map/ppermute | solution.py:14
  84.2 0.5 fusion.10
  84.7 0.7 multiply_convert_fusion.2
  85.4 1.0 fusion.30
  86.4 1.3 convolution_bitcast_fusion
  87.7 1.3 fusion.22
  89.0 0.0 all-reduce.5.cloned.1.call-update
  89.0 0.0 all-reduce.7.cloned.1.call-start
  89.0 471.6 %all-reduce.5.cloned.1.call-done = (f32[256,512]{1,0:T(8,128)}, f32[256,512]{1,0:T(8,128)}, f32[256,256]{1,0:T(8,128)}, f32[256,512]{1,0:T(8,128)}, f32[256,512]{1,0:T(8,128)}, /*index=5*/f32[256,256]{1,0:T(8,128)}) async-done(((f32[256,512]{1,0:T(8,128)}, f32[256,512]{1,0:T(8,128)}, f32[256,256]{1,0:T(8,128)}, f32[256,512]{1,0:T(8,128)}, f32[256,512]{1,0:T(8,128)}, /*index=5*/f32[256,256]{1,0:T(8,128)}), ...) | async-done | bytes 2621456 | tf_op jit(solution)/shard_map/psum | solution.py:61
  560.6 0.0 all-reduce.7.cloned.1.call-update
  560.7 0.0 copy-start.6
  560.7 0.5 fusion.3
  561.2 3.1 collective-permute-start.3
  564.3 3.9 collective-permute-done.3
  568.2 1.3 fusion.11
  569.5 101.2 %all-reduce.7.cloned.1.call-done = (f32[256,512]{1,0:T(8,128)}, f32[256,512]{1,0:T(8,128)}, f32[256,256]{1,0:T(8,128)}, f32[256,512]{1,0:T(8,128)}, f32[256,512]{1,0:T(8,128)}, /*index=5*/f32[256,256]{1,0:T(8,128)}) async-done(((f32[256,512]{1,0:T(8,128)}, f32[256,512]{1,0:T(8,128)}, f32[256,256]{1,0:T(8,128)}, f32[256,512]{1,0:T(8,128)}, f32[256,512]{1,0:T(8,128)}, /*index=5*/f32[256,256]{1,0:T(8,128)}), ...) | async-done | bytes 2621456 | tf_op jit(solution)/shard_map/psum | solution.py:61
  670.7 2.2 multiply_convert_fusion.9
  672.9 1.8 multiply_convert_fusion.11
  674.7 0.0 copy-done.2
  674.7 0.9 multiply_convert_fusion.7
  (9 shorter events, 0.1 us)
Async XLA Ops:
  7.2 53.4 %copy-start = (bf16[256,512]{1,0:T(8,128)(2,1)S(1)}, bf16[256,512]{1,0:T(8,128)(2,1)}, u32[]{:S(2)}) copy-start(bf16[256,512]{1,0:T(8,128)(2,1)} %param.13) | copy-start | bytes 786436
  7.2 8.9 %copy-start.4 = (bf16[256,512]{1,0:T(8,128)(2,1)S(1)}, bf16[256,512]{1,0:T(8,128)(2,1)}, u32[]{:S(2)}) copy-start(bf16[256,512]{1,0:T(8,128)(2,1)} %param.10) | copy-start | bytes 786436
  7.2 553.5 %all-reduce.5.cloned.1.call-start = ((), (), s32[]{:S(2)}) async-start(), calls=%async_computation | async-start | bytes 5242880 | tf_op jit(solution)/shard_map/psum | solution.py:61
  8.4 7.7 %collective-permute-start = (bf16[1,512,256]{2,1,0:T(8,128)(2,1)S(1)}, bf16[1,512,256]{2,1,0:T(8,128)(2,1)S(1)}, u32[]{:S(2)}, u32[]{:S(2)}) collective-permute-start(bf16[1,512,256]{2,1,0:T(8,128)(2,1)S(1)} %get-tuple-element.25), channel_id=1, source_target_pairs={{0,1},{1,2},{2,3},{3,4},{4,5},{5,6},{6,7},{7,8},{8,9},{9,10},{10,1... | collective-permute-start | bytes 786440 | tf_op jit(solution)/shard_map/ppermute | solution.py:14
  16.6 1.0 copy-start.1
  16.6 1.1 copy-start.7
  16.6 10.5 %copy-start.5 = (bf16[256,512]{1,0:T(8,128)(2,1)S(1)}, bf16[256,512]{1,0:T(8,128)(2,1)}, u32[]{:S(2)}) copy-start(bf16[256,512]{1,0:T(8,128)(2,1)} %param.14) | copy-start | bytes 786436
  18.0 42.6 %collective-permute-start.1 = (bf16[1,1024,256]{2,1,0:T(8,128)(2,1)S(1)}, bf16[1,1024,256]{2,1,0:T(8,128)(2,1)S(1)}, u32[]{:S(2)}, u32[]{:S(2)}) collective-permute-start(bf16[1,1024,256]{2,1,0:T(8,128)(2,1)S(1)} %bitcast.60), channel_id=1, source_target_pairs={{0,8},{1,9},{2,10},{3,11},{4,12},{5,13},{6,14},{7,15},{8,16},{9,17... | collective-permute-start | bytes 1572872 | tf_op jit(solution)/shard_map/ppermute | solution.py:14
  27.6 33.5 %copy-start.8 = (bf16[1,1024,256]{2,1,0:T(8,128)(2,1)S(1)}, bf16[1,1024,256]{2,1,0:T(8,128)(2,1)}, u32[]{:S(2)}) copy-start(bf16[1,1024,256]{2,1,0:T(8,128)(2,1)} %param.9) | copy-start | bytes 1572868
  27.6 33.5 %copy-start.9 = (bf16[256,256]{1,0:T(8,128)(2,1)S(1)}, bf16[256,256]{1,0:T(8,128)(2,1)}, u32[]{:S(2)}) copy-start(bf16[256,256]{1,0:T(8,128)(2,1)} %param.15) | copy-start | bytes 393220
  63.6 20.6 %collective-permute-start.2 = (bf16[1,1024,256]{2,1,0:T(8,128)(2,1)S(1)}, bf16[1,1024,256]{2,1,0:T(8,128)(2,1)S(1)}, u32[]{:S(2)}, u32[]{:S(2)}) collective-permute-start(bf16[1,1024,256]{2,1,0:T(8,128)(2,1)S(1)} %fusion.2), channel_id=1, source_target_pairs={{8,0},{9,1},{10,2},{11,3},{12,4},{13,5},{14,6},{15,7},{16,8},{17,9... | collective-permute-start | bytes 1572872 | tf_op jit(solution)/shard_map/ppermute | solution.py:14
  89.0 581.7 %all-reduce.7.cloned.1.call-start = ((), (), s32[]{:S(2)}) async-start(), calls=%async_computation.1 | async-start | bytes 5242880 | tf_op jit(solution)/shard_map/psum | solution.py:61
  560.7 7.5 %copy-start.6 = (bf16[256,512]{1,0:T(8,128)(2,1)S(1)}, bf16[256,512]{1,0:T(8,128)(2,1)}, u32[]{:S(2)}) copy-start(bf16[256,512]{1,0:T(8,128)(2,1)} %param.11) | copy-start | bytes 786436
  561.2 7.0 %collective-permute-start.3 = (bf16[1,512,256]{2,1,0:T(8,128)(2,1)S(1)}, bf16[1,512,256]{2,1,0:T(8,128)(2,1)S(1)}, u32[]{:S(2)}, u32[]{:S(2)}) collective-permute-start(bf16[1,512,256]{2,1,0:T(8,128)(2,1)S(1)} %get-tuple-element.24), channel_id=1, source_target_pairs={{1,0},{2,1},{3,2},{4,3},{5,4},{6,5},{7,6},{8,7},{9,8},{10,9},{11,1... | collective-permute-start | bytes 786440 | tf_op jit(solution)/shard_map/ppermute | solution.py:14
  670.7 4.0 copy-start.2
  670.7 4.0 copy-start.3
Sparse Core Ops, SparseCore 0:
  89.1 471.4 all-reduce.4
  564.4 106.2 all-reduce.6
